TPU v7x, 32 devices: a whole 2x2x4 slice. The times are simulated.
32 devices in a mesh: aux: 4 (over y, x), pair: 8 (over z, core).
Axes of the slice: x: 2, y: 2, z: 4, core: 2. Of those that a mesh axis runs over, the one named last changes fastest.
Arguments:
- three_index: bfloat16 [32, 2048, 256], P('pair', 'aux'), may hold values from -6 to 6
- pno_coef: bfloat16 [128, 2, 256, 192], P('pair'), may hold values from -0.375 to 0.375
- pair_orbitals: int32 [128, 2], P('pair'), may hold values from 0 to 31, as said below
- natural_orbital_class: int32 [128], P('pair'), may hold values from 0 to 3
- pno_energy: float32 [128, 192], P('pair'), may hold values from 0.5 to 4
- margin: bfloat16 [128, 2, 192, 192], P('pair'), may hold values from -0.4375 to 0.4375
- neighbour_pairs: int32 [128, 2], P('pair'), may hold values from 0 to 127, as said below
- fock_coupling: float32 [128, 2], P('pair'), may hold values from -0.9 to 0.9
Outputs:
- amplitudes: float32 [128, 192, 192], P('pair')
- residual: float32 [128, 192, 192], P('pair')
Inputs may be any that keep to these rules, and one draw needn't show every extreme that they name: `pair_orbitals`: column 0 names an orbital of the pair's own block of 4 orbitals (pair p's block is p // 16); column 1 names one of that block or of the block just before or after it. `neighbour_pairs`: each entry names another pair of the pair's own block of 16 pairs or of the block just before or after it.
All inputs are finite; a program needn't handle non-finite values.
Results may differ from a plain program's by a relative error of at most 0.0032.
Values may be sent and summed in bfloat16 or wider, within the bound.
No kernel may reach another device: no remote copies, remote signals or barrier semaphores. Data moves between devices by JAX's collectives and lax.ppermute only.
A program may use at most 128 MiB of HBM per device.

v0:
```python
import jax
import jax.numpy as jnp
from jax import lax
from jax.sharding import PartitionSpec as P

NPNO = 192
ITERS = 2


def with_halo(cells, sides, width):
    for axis, dim in sides:
        count = lax.axis_size(axis)
        ends = count - 1
        head = lax.slice_in_dim(cells, 0, width, axis=dim)
        tail = lax.slice_in_dim(cells, cells.shape[dim] - width, cells.shape[dim], axis=dim)
        cells = jnp.concatenate(
            [
                lax.ppermute(tail, axis, [(i, (i + 1) % count) for i in range(ends)]),
                cells,
                lax.ppermute(head, axis, [((i + 1) % count, i) for i in range(ends)]),
            ],
            axis=dim,
        )
    return cells


def class_mask(natural_orbital_class):
    counts = jnp.where(
        natural_orbital_class == 0,
        NPNO // 6,
        jnp.where(
            natural_orbital_class == 1,
            NPNO // 3,
            jnp.where(natural_orbital_class == 2, 2 * NPNO // 3, NPNO),
        ),
    )
    return jnp.arange(NPNO, dtype=jnp.int32)[None, :] < counts[:, None]


def transformed_product(side_blocks, gathered, weights):
    inner_part = jnp.einsum(
        "pnab,pnbc->pnac", side_blocks, gathered, precision=lax.Precision.HIGHEST
    )
    outer_part = jnp.einsum(
        "pnac,pndc->pnad", inner_part, side_blocks, precision=lax.Precision.HIGHEST
    )
    return jnp.einsum("pn,pnad->pad", weights, outer_part, precision=lax.Precision.HIGHEST)


def iterate(exchange_ints, denominator, coupling):
    amplitudes = jnp.zeros_like(exchange_ints)
    for iteration in range(ITERS):
        current_residual = exchange_ints + denominator * amplitudes
        if iteration > 0:
            current_residual = current_residual - coupling(amplitudes)
        amplitudes = amplitudes - current_residual / denominator
    residual = exchange_ints + denominator * amplitudes - coupling(amplitudes)
    return (amplitudes, residual)


def per_device(
    three_index,
    pno_coef,
    pair_orbitals,
    natural_orbital_class,
    pno_energy,
    margin,
    neighbour_pairs,
    fock_coupling,
):
    occ_dev = three_index.shape[0]
    pair_dev = pno_coef.shape[0]
    position = lax.axis_index("pair")
    natural_orbital_mask = class_mask(natural_orbital_class)
    padded = with_halo(three_index, (("pair", 0),), occ_dev)
    local_orbitals = pair_orbitals - (position - 1) * occ_dev
    leading_block = jnp.take(padded, local_orbitals[:, 0], axis=0)
    trailing_block = jnp.take(padded, local_orbitals[:, 1], axis=0)
    masked_coefficient_rows = jnp.where(
        natural_orbital_mask[:, None, None, :], pno_coef, jnp.zeros((), jnp.bfloat16)
    )
    left_half = jnp.einsum(
        "cyg,cgh->cyh",
        leading_block,
        masked_coefficient_rows[:, 0],
        preferred_element_type=jnp.float32,
    ).astype(jnp.bfloat16)
    right_half = jnp.einsum(
        "cyg,cgh->cyh",
        trailing_block,
        masked_coefficient_rows[:, 1],
        preferred_element_type=jnp.float32,
    ).astype(jnp.bfloat16)
    partial_ints = jnp.einsum(
        "pqa,pqb->pab", left_half, right_half, preferred_element_type=jnp.float32
    )
    mask_float = natural_orbital_mask.astype(jnp.float32)
    exchange_ints = lax.psum(partial_ints, "aux")
    denominator = pno_energy[:, :, None] + pno_energy[:, None, :]
    side_blocks = margin.astype(jnp.float32) * mask_float[:, None, :, None]
    local_rows = neighbour_pairs - (position - 1) * pair_dev

    def coupling(current):
        padded_amps = with_halo(current, (("pair", 0),), pair_dev)
        gathered = jnp.take(padded_amps, local_rows, axis=0)
        return transformed_product(side_blocks, gathered, fock_coupling)

    amplitudes, residual = iterate(exchange_ints, denominator, coupling)
    return (amplitudes, residual)


def solution(mesh):
    return jax.shard_map(
        per_device,
        mesh=mesh,
        in_specs=(
            P("pair", "aux", None),
            P("pair", None, None, None),
            P("pair", None),
            P("pair"),
            P("pair", None),
            P("pair", None, None, None),
            P("pair", None),
            P("pair", None),
        ),
        out_specs=(P("pair", None, None), P("pair", None, None)),
        check_vma=False,
    )
```

profile of v0, /device:TPU:1, one launch (start us, length us, event | category | flops | bytes accessed | tf_op | source)
XLA Modules:
  0.0 342.3 jit_solution(12701743786358412983)
XLA Ops:
  7.2 0.0 all-reduce.2.cloned.1.call-start
  7.2 4.6 %collective-permute-start = (bf16[4,512,256]{2,1,0:T(8,128)(2,1)}, bf16[4,512,256]{2,1,0:T(8,128)(2,1)}, u32[]{:S(2)}, u32[]{:S(2)}) collective-permute-start(bf16[4,512,256]{2,1,0:T(8,128)(2,1)} %param.12), channel_id=1, source_target_pairs={{0,1},{1,2},{2,3},{3,4},{4,5},{5,6},{6,7},{8,9},{9,10},{10,11},{11... | collective-permute-start | bytes 3145736 | tf_op jit(solution)/shard_map/ppermute | solution.py:18
  11.8 1.9 collective-permute-start.1
  13.8 0.7 broadcast_subtract_fusion
  14.4 0.7 compare_select_fusion.5
  15.1 0.1 fusion.45
  15.2 0.0 copy-start.7
  15.2 3.4 %broadcast_select_fusion = bf16[16,2,256,192]{2,3,1,0:T(8,128)(2,1)} fusion(bf16[16,2,256,192]{2,3,1,0:T(8,128)(2,1)} %param.13, pred[16,192]{1,0:T(8,128)(4,1)S(1)} %get-tuple-element.13), kind=kLoop, calls=%fused_computation.46 | loop fusion | flops 1572864 | bytes 6294528 | tf_op jit(solution)/shard_map/jit(_where)/select_n | solution.py:79
  18.6 5.2 %collective-permute-done = bf16[4,512,256]{2,1,0:T(8,128)(2,1)} collective-permute-done((bf16[4,512,256]{2,1,0:T(8,128)(2,1)}, bf16[4,512,256]{2,1,0:T(8,128)(2,1)}, u32[]{:S(2)}, u32[]{:S(2)}) %collective-permute-start) | collective-permute-done | bytes 1048608 | tf_op jit(solution)/shard_map/ppermute | solution.py:18
  23.9 1.3 constant_dynamic-update-slice_fusion.2
  25.1 0.0 copy-done.7
  25.2 0.1 constant_dynamic-update-slice_fusion.1
  25.2 3.0 collective-permute-done.1
  28.3 1.3 constant_dynamic-update-slice_fusion
  29.6 2.8 gather_fusion.1
  32.3 2.8 gather_fusion
  35.1 0.0 copy-start.6
  35.1 6.1 %fusion.10 = bf16[16,512,192]{1,2,0:T(8,128)(2,1)} fusion(bf16[16,512,256]{2,1,0:T(8,128)(2,1)} %gather_fusion.1, pred[16]{0:T(512)(128)(4,1)S(1)} %get-tuple-element.10, bf16[16,2,256,192]{2,3,1,0:T(8,128)(2,1)} %broadcast_select_fusion), kind=kOutput, calls=%fused_computation.22 | convolution fusion | flops 807403520 | bytes 8912912 | tf_op jit(solution)/shard_map/cyg,cgh->cyh/dot_general | solution.py:88
  41.2 0.0 copy-done.6
  41.2 7.3 %fusion.29 = f32[16,192,192]{2,1,0:T(8,128)} fusion(bf16[16,512,192]{1,2,0:T(8,128)(2,1)} %fusion.10, bf16[16,512,256]{2,1,0:T(8,128)(2,1)} %gather_fusion, pred[16]{0:T(512)(128)(4,1)S(1)} %get-tuple-element.6, bf16[16,2,256,192]{2,3,1,0:T(8,128)(2,1)S(1)} %copy-done.6), kind=kOutput, calls=%fused_computation.41 | convolution fusion | flops 1412956160 | bytes 11272704 | tf_op jit(solution)/shard_map/pqa,pqb->pab/dot_general | solution.py:94
  48.5 0.0 copy-start.8
  48.5 0.0 all-reduce.2.cloned.1.call-update
  48.5 0.0 copy-start.9
  48.5 0.0 copy-start.10
  48.5 87.1 %all-reduce.2.cloned.1.call-done = f32[16,192,192]{2,1,0:T(8,128)} async-done(((f32[16,192,192]{2,1,0:T(8,128)}), f32[16,192,192]{2,1,0:T(8,128)}) %all-reduce.2.cloned.1.call-update) | async-done | bytes 2359312 | tf_op jit(solution)/shard_map/psum | solution.py:98
  135.6 0.0 copy-done.8
  135.6 2.3 fusion.17
  137.9 2.6 collective-permute-start.3
  140.5 3.5 %collective-permute-start.2 = (f32[16,192,192]{2,1,0:T(8,128)S(1)}, f32[16,192,192]{2,1,0:T(8,128)}, u32[]{:S(2)}, u32[]{:S(2)}) collective-permute-start(f32[16,192,192]{2,1,0:T(8,128)S(1)} %fusion.17), channel_id=1, source_target_pairs={{0,1},{1,2},{2,3},{3,4},{4,5},{5,6},{6,7},{8,9},{9,10},{10,11},{11... | collective-permute-start | bytes 7077896 | tf_op jit(solution)/shard_map/ppermute | solution.py:18
  144.0 0.0 copy-done.9
  144.1 0.1 copy.14
  144.2 0.0 copy-done.10
  144.2 0.1 copy.19
  144.3 0.1 copy.15
  144.3 0.1 reshape.94
  144.4 32.2 %collective-permute-done.3 = f32[16,192,192]{2,1,0:T(8,128)} collective-permute-done((f32[16,192,192]{2,1,0:T(8,128)S(1)}, f32[16,192,192]{2,1,0:T(8,128)}, u32[]{:S(2)}, u32[]{:S(2)}) %collective-permute-start.3) | collective-permute-done | bytes 2359328 | tf_op jit(solution)/shard_map/ppermute | solution.py:20
  176.6 1.1 collective-permute-done.2
  177.7 7.4 %pad_maximum_fusion = f32[48,192,192]{2,1,0:T(8,128)} fusion(f32[16,192,192]{2,1,0:T(8,128)} %collective-permute-done.3, f32[16,192,192]{2,1,0:T(8,128)S(1)} %fusion.17, f32[16,192,192]{2,1,0:T(8,128)} %collective-permute-done.2), kind=kLoop, calls=%fused_computation.4 | loop fusion | flops 3538944 | bytes 14155776 | tf_op jit(solution)/shard_map/concatenate | solution.py:16
  185.2 0.0 copy-start
  185.2 7.5 %gather_fusion.2 = f32[32,192,192]{2,1,0:T(8,128)} fusion(f32[48,192,192]{2,1,0:T(8,128)} %pad_maximum_fusion, s32[1024]{0:T(1024)S(1)} %pad_clamp_fusion), kind=kCustom, calls=%fused_computation.1.clone | custom fusion | bytes 9437312 | tf_op jit(solution)/shard_map/jit(_take)/gather | solution.py:105
  192.6 0.0 copy-done
  192.6 9.5 %fusion.2 = f32[16,2,192,192]{3,2,1,0:T(8,128)S(1)} fusion(f32[16,2,192,192]{3,2,1,0:T(8,128)} %bitcast.26, bf16[16,2,192,192]{3,2,1,0:T(8,128)(2,1)S(1)} %copy-done, f32[16,192]{1,0:T(8,128)S(1)} %get-tuple-element.12, pred[16,2]{1,0:T(8,128)(4,1)S(1)} %copy.14), kind=kOutput, calls=%fused_computation.13 | convolution fusion | flops 2721447936 | bytes 11808800 | tf_op jit(solution)/shard_map/pnab,pnbc->pnac/dot_general | solution.py:41
  202.2 8.0 %fusion.5 = f32[16,2,192,192]{3,2,1,0:T(8,128)S(1)} fusion(f32[16,2,192,192]{3,2,1,0:T(8,128)S(1)} %fusion.2, bf16[16,2,192,192]{3,2,1,0:T(8,128)(2,1)S(1)} %copy-done, f32[16,192]{1,0:T(8,128)S(1)} %get-tuple-element.12), kind=kOutput, calls=%fused_computation.17 | convolution fusion | flops 2720268288 | bytes 11808768 | tf_op jit(solution)/shard_map/pnac,pndc->pnad/dot_general | solution.py:44
  210.2 0.0 copy-start.3
  210.2 23.3 %fusion.8 = f32[16,1,192,192]{3,1,2,0:T(1,128)S(1)} fusion(f32[16,2,1,1]{1,2,3,0:T(1,128)S(1)} %copy.19, f32[16,2,192,192]{3,2,1,0:T(8,128)S(1)} %fusion.5), kind=kOutput, calls=%fused_computation.20 | convolution fusion | flops 14155776 | bytes 7078016 | tf_op jit(solution)/shard_map/pn,pnad->pad/dot_general | solution.py:47
  233.6 0.0 copy-done.3
  233.6 1.4 fusion.20
  235.0 0.0 copy-start.1
  235.0 1.9 collective-permute-start.5
  236.9 0.0 copy-done.1
  236.9 4.5 %collective-permute-start.4 = (f32[16,192,192]{2,1,0:T(8,128)S(1)}, f32[16,192,192]{2,1,0:T(8,128)}, u32[]{:S(2)}, u32[]{:S(2)}) collective-permute-start(f32[16,192,192]{2,1,0:T(8,128)S(1)} %fusion.20), channel_id=1, source_target_pairs={{0,1},{1,2},{2,3},{3,4},{4,5},{5,6},{6,7},{8,9},{9,10},{10,11},{11... | collective-permute-start | bytes 7077896 | tf_op jit(solution)/shard_map/ppermute | solution.py:18
  241.4 33.0 %collective-permute-done.5 = f32[16,192,192]{2,1,0:T(8,128)S(1)} collective-permute-done((f32[16,192,192]{2,1,0:T(8,128)S(1)}, f32[16,192,192]{2,1,0:T(8,128)S(1)}, u32[]{:S(2)}, u32[]{:S(2)}) %collective-permute-start.5) | collective-permute-done | bytes 2359328 | tf_op jit(solution)/shard_map/ppermute | solution.py:20
  274.4 1.7 copy-done.5
  276.1 0.0 collective-permute-done.4
  276.1 8.5 %pad_maximum_fusion.1 = f32[48,192,192]{2,1,0:T(8,128)} fusion(f32[16,192,192]{2,1,0:T(8,128)} %copy-done.5, f32[16,192,192]{2,1,0:T(8,128)} %copy-done.1, f32[16,192,192]{2,1,0:T(8,128)} %collective-permute-done.4), kind=kLoop, calls=%fused_computation.5 | loop fusion | flops 3538944 | bytes 14155776 | tf_op jit(solution)/shard_map/concatenate | solution.py:16
  284.6 7.3 %gather_fusion.3 = f32[32,192,192]{2,1,0:T(8,128)} fusion(f32[48,192,192]{2,1,0:T(8,128)} %pad_maximum_fusion.1, s32[1024]{0:T(1024)S(1)} %pad_clamp_fusion), kind=kCustom, calls=%fused_computation.3.clone | custom fusion | bytes 9437312 | tf_op jit(solution)/shard_map/jit(_take)/gather | solution.py:105
  291.9 9.7 %fusion = f32[16,2,192,192]{3,2,1,0:T(8,128)S(1)} fusion(f32[16,2,192,192]{3,2,1,0:T(8,128)} %bitcast.25, bf16[16,2,192,192]{3,2,1,0:T(8,128)(2,1)S(1)} %copy-done, f32[16,192]{1,0:T(8,128)S(1)} %get-tuple-element.12, pred[16,2]{1,0:T(8,128)(4,1)S(1)} %copy.14), kind=kOutput, calls=%fused_computation.11 | convolution fusion | flops 2721447936 | bytes 11808800 | tf_op jit(solution)/shard_map/pnab,pnbc->pnac/dot_general | solution.py:41
  301.7 8.0 %fusion.4 = f32[16,2,192,192]{3,2,1,0:T(8,128)S(1)} fusion(f32[16,2,192,192]{3,2,1,0:T(8,128)S(1)} %fusion, bf16[16,2,192,192]{3,2,1,0:T(8,128)(2,1)S(1)} %copy-done, f32[16,192]{1,0:T(8,128)S(1)} %get-tuple-element.12), kind=kOutput, calls=%fused_computation.16 | convolution fusion | flops 2720268288 | bytes 11808768 | tf_op jit(solution)/shard_map/pnac,pndc->pnad/dot_general | solution.py:44
  309.7 0.0 copy-start.2
  309.7 0.0 copy-start.4
  309.7 23.4 %fusion.6 = f32[16,1,192,192]{3,1,2,0:T(1,128)S(1)} fusion(f32[16,2,1,1]{1,2,3,0:T(1,128)S(1)} %copy.19, f32[16,2,192,192]{3,2,1,0:T(8,128)S(1)} %fusion.4), kind=kOutput, calls=%fused_computation.18 | convolution fusion | flops 14155776 | bytes 7078016 | tf_op jit(solution)/shard_map/pn,pnad->pad/dot_general | solution.py:47
  333.2 0.0 copy-done.2
  333.2 0.0 copy-done.4
  333.2 2.0 fusion.22
  (5 shorter events, 0.0 us)
Async XLA Ops:
  7.2 128.4 %all-reduce.2.cloned.1.call-start = ((), (), s32[]{:S(2)}) async-start(), calls=%async_computation | async-start | bytes 6291456 | tf_op jit(solution)/shard_map/psum | solution.py:98
  7.2 16.6 %collective-permute-start = (bf16[4,512,256]{2,1,0:T(8,128)(2,1)}, bf16[4,512,256]{2,1,0:T(8,128)(2,1)}, u32[]{:S(2)}, u32[]{:S(2)}) collective-permute-start(bf16[4,512,256]{2,1,0:T(8,128)(2,1)} %param.12), channel_id=1, source_target_pairs={{0,1},{1,2},{2,3},{3,4},{4,5},{5,6},{6,7},{8,9},{9,10},{10,11},{11... | collective-permute-start | bytes 3145736 | tf_op jit(solution)/shard_map/ppermute | solution.py:18
  11.8 16.4 %collective-permute-start.1 = (bf16[4,512,256]{2,1,0:T(8,128)(2,1)}, bf16[4,512,256]{2,1,0:T(8,128)(2,1)}, u32[]{:S(2)}, u32[]{:S(2)}) collective-permute-start(bf16[4,512,256]{2,1,0:T(8,128)(2,1)} %param.12), channel_id=1, source_target_pairs={{1,0},{2,1},{3,2},{4,3},{5,4},{6,5},{7,6},{9,8},{10,9},{11,10},{12... | collective-permute-start | bytes 3145736 | tf_op jit(solution)/shard_map/ppermute | solution.py:20
  15.2 10.0 %copy-start.7 = (bf16[4,512,256]{2,1,0:T(8,128)(2,1)S(1)}, bf16[4,512,256]{2,1,0:T(8,128)(2,1)}, u32[]{:S(2)}) copy-start(bf16[4,512,256]{2,1,0:T(8,128)(2,1)} %param.12) | copy-start | bytes 3145732
  35.1 6.1 %copy-start.6 = (bf16[16,2,256,192]{2,3,1,0:T(8,128)(2,1)S(1)}, bf16[16,2,256,192]{2,3,1,0:T(8,128)(2,1)}, u32[]{:S(2)}) copy-start(bf16[16,2,256,192]{2,3,1,0:T(8,128)(2,1)} %broadcast_select_fusion) | copy-start | bytes 9437188
  48.5 87.1 %copy-start.8 = (f32[16,192]{1,0:T(8,128)S(1)}, f32[16,192]{1,0:T(8,128)}, u32[]{:S(2)}) copy-start(f32[16,192]{1,0:T(8,128)} %param.16) | copy-start | bytes 36868
  48.5 95.5 %copy-start.9 = (s32[16,2]{0,1:T(2,128)S(1)}, s32[16,2]{0,1:T(2,128)}, u32[]{:S(2)}) copy-start(s32[16,2]{0,1:T(2,128)} %param.18) | copy-start | bytes 388
  48.5 95.7 %copy-start.10 = (f32[16,2]{0,1:T(2,128)S(1)}, f32[16,2]{0,1:T(2,128)}, u32[]{:S(2)}) copy-start(f32[16,2]{0,1:T(2,128)} %param.19) | copy-start | bytes 388
  137.9 38.7 %collective-permute-start.3 = (f32[16,192,192]{2,1,0:T(8,128)S(1)}, f32[16,192,192]{2,1,0:T(8,128)}, u32[]{:S(2)}, u32[]{:S(2)}) collective-permute-start(f32[16,192,192]{2,1,0:T(8,128)S(1)} %fusion.17), channel_id=1, source_target_pairs={{1,0},{2,1},{3,2},{4,3},{5,4},{6,5},{7,6},{9,8},{10,9},{11,10},{12... | collective-permute-start | bytes 7077896 | tf_op jit(solution)/shard_map/ppermute | solution.py:20
  140.5 37.2 %collective-permute-start.2 = (f32[16,192,192]{2,1,0:T(8,128)S(1)}, f32[16,192,192]{2,1,0:T(8,128)}, u32[]{:S(2)}, u32[]{:S(2)}) collective-permute-start(f32[16,192,192]{2,1,0:T(8,128)S(1)} %fusion.17), channel_id=1, source_target_pairs={{0,1},{1,2},{2,3},{3,4},{4,5},{5,6},{6,7},{8,9},{9,10},{10,11},{11... | collective-permute-start | bytes 7077896 | tf_op jit(solution)/shard_map/ppermute | solution.py:18
  185.2 7.5 %copy-start = (bf16[16,2,192,192]{3,2,1,0:T(8,128)(2,1)S(1)}, bf16[16,2,192,192]{3,2,1,0:T(8,128)(2,1)}, u32[]{:S(2)}) copy-start(bf16[16,2,192,192]{3,2,1,0:T(8,128)(2,1)} %param.17) | copy-start | bytes 7077892
  210.2 23.4 %copy-start.3 = (f32[16,192,192]{2,1,0:T(8,128)S(1)}, f32[16,192,192]{2,1,0:T(8,128)}, u32[]{:S(2)}) copy-start(f32[16,192,192]{2,1,0:T(8,128)} %all-reduce.2.cloned.1.call-done) | copy-start | bytes 7077892
  235.0 1.9 copy-start.1
  235.0 39.4 %collective-permute-start.5 = (f32[16,192,192]{2,1,0:T(8,128)S(1)}, f32[16,192,192]{2,1,0:T(8,128)S(1)}, u32[]{:S(2)}, u32[]{:S(2)}) collective-permute-start(f32[16,192,192]{2,1,0:T(8,128)S(1)} %fusion.20), channel_id=1, source_target_pairs={{1,0},{2,1},{3,2},{4,3},{5,4},{6,5},{7,6},{9,8},{10,9},{11,10},{12... | collective-permute-start | bytes 7077896 | tf_op jit(solution)/shard_map/ppermute | solution.py:20
  236.9 39.2 %collective-permute-start.4 = (f32[16,192,192]{2,1,0:T(8,128)S(1)}, f32[16,192,192]{2,1,0:T(8,128)}, u32[]{:S(2)}, u32[]{:S(2)}) collective-permute-start(f32[16,192,192]{2,1,0:T(8,128)S(1)} %fusion.20), channel_id=1, source_target_pairs={{0,1},{1,2},{2,3},{3,4},{4,5},{5,6},{6,7},{8,9},{9,10},{10,11},{11... | collective-permute-start | bytes 7077896 | tf_op jit(solution)/shard_map/ppermute | solution.py:18
  274.4 1.7 copy-start.5
  309.7 23.5 %copy-start.2 = (f32[16,192,192]{2,1,0:T(8,128)S(1)}, f32[16,192,192]{2,1,0:T(8,128)}, u32[]{:S(2)}) copy-start(f32[16,192,192]{2,1,0:T(8,128)} %copy-done.1) | copy-start | bytes 7077892
  309.7 23.5 %copy-start.4 = (f32[16,192,192]{2,1,0:T(8,128)S(1)}, f32[16,192,192]{2,1,0:T(8,128)}, u32[]{:S(2)}) copy-start(f32[16,192,192]{2,1,0:T(8,128)} %all-reduce.2.cloned.1.call-done) | copy-start | bytes 7077892
Sparse Core Ops, SparseCore 0:
  48.6 86.9 all-reduce.1
where the time goes:
time: 347 us; the launch traced here: 342 us
  waiting for transfers between devices  162 us (47%)
  matrix products  95.5 us (28%)
  other arithmetic  26.6 us (8%)
  local copies, waits for them, and re-layouts  25 us (7%)
  starting transfers between devices  19.1 us (6%)
  between operations  14.6 us (4%)
    psum x1, waiting for transfers between devices, per_device(): exchange_ints = lax.psum(partial_ints, 'aux')  87.1 us
    ppermute x3, waiting for transfers between devices, with_halo(): lax.ppermute(head, axis, [((i + 1) % count, i) for i in range(ends)])  68.2 us
    dot_general x2, matrix products, transformed_product(): jnp.einsum('pn,pnad->pad', weights, outer_part, precision=lax.Precision.H...  46.8 us
    dot_general x2, matrix products, transformed_product(): jnp.einsum('pnab,pnbc->pnac', side_blocks, gathered, precision=lax.Precis...  19.3 us
    dot_general x2, matrix products, transformed_product(): jnp.einsum('pnac,pndc->pnad', inner_part, side_blocks, precision=lax.Prec...  16.1 us
    concatenate x2, other arithmetic, with_halo(): jnp.concatenate([lax.ppermute(tail, axis, [(i, (i + 1) % count) for i in...  16 us
    gather x2, local copies, waits for them, and re-layouts, coupling(): gathered = jnp.take(padded_amps, local_rows, axis=0)  14.8 us
    ppermute x3, starting transfers between devices, with_halo(): lax.ppermute(tail, axis, [(i, (i + 1) % count) for i in range(ends)])  12.6 us
  transfers between devices with their start and end apart: 7, of which 6 were waited for; matrix products, arithmetic and copies ran while one was open for 2% of the time, Pallas kernels for 0%

commit v1 on v0

--- a/solution.py
+++ b/solution.py
@@ -95,7 +95,7 @@
         "pqa,pqb->pab", left_half, right_half, preferred_element_type=jnp.float32
     )
     mask_float = natural_orbital_mask.astype(jnp.float32)
-    exchange_ints = lax.psum(partial_ints, "aux")
+    exchange_ints = jnp.sum(lax.all_gather(partial_ints, "aux"), axis=0)
     denominator = pno_energy[:, :, None] + pno_energy[:, None, :]
     side_blocks = margin.astype(jnp.float32) * mask_float[:, None, :, None]
     local_rows = neighbour_pairs - (position - 1) * pair_dev

time: 347 us -> 390 us (1.12)
  waiting for transfers between devices: 162 us -> 198 us
  other arithmetic: 26.6 us -> 33.1 us
    all_gather x0 -> x1, waiting for transfers between devices: none -> 122 us  [per_device(): exchange_ints = jnp.sum(lax.all_gather(partial_ints, 'aux'), axis=0)]
    psum x1 -> x0, waiting for transfers between devices: 87.1 us -> none  [per_device(): exchange_ints = lax.psum(partial_ints, 'aux')]
    reduce_sum x0 -> x1, other arithmetic: none -> 6.19 us  [per_device(): exchange_ints = jnp.sum(lax.all_gather(partial_ints, 'aux'), axis=0)]
where the time goes in v1:
time: 390 us; the launch traced here: 385 us
  waiting for transfers between devices  198 us (51%)
  matrix products  95.6 us (25%)
  other arithmetic  33.1 us (8%)
  local copies, waits for them, and re-layouts  25.3 us (6%)
  starting transfers between devices  18.5 us (5%)
  between operations  14.5 us (4%)
    all_gather x1, waiting for transfers between devices, per_device(): exchange_ints = jnp.sum(lax.all_gather(partial_ints, 'aux'), axis=0)  122 us
    ppermute x3, waiting for transfers between devices, with_halo(): lax.ppermute(head, axis, [((i + 1) % count, i) for i in range(ends)])  68.8 us
    dot_general x2, matrix products, transformed_product(): jnp.einsum('pn,pnad->pad', weights, outer_part, precision=lax.Precision.H...  46.7 us
    dot_general x2, matrix products, transformed_product(): jnp.einsum('pnab,pnbc->pnac', side_blocks, gathered, precision=lax.Precis...  19.4 us
    concatenate x2, other arithmetic, with_halo(): jnp.concatenate([lax.ppermute(tail, axis, [(i, (i + 1) % count) for i in...  16.2 us
    dot_general x2, matrix products, transformed_product(): jnp.einsum('pnac,pndc->pnad', inner_part, side_blocks, precision=lax.Prec...  16.1 us
    gather x2, local copies, waits for them, and re-layouts, coupling(): gathered = jnp.take(padded_amps, local_rows, axis=0)  14.7 us
    ppermute x3, starting transfers between devices, with_halo(): lax.ppermute(tail, axis, [(i, (i + 1) % count) for i in range(ends)])  12.1 us
  transfers between devices with their start and end apart: 7, of which 6 were waited for; matrix products, arithmetic and copies ran while one was open for 2% of the time, Pallas kernels for 0%

profile of v1, /device:TPU:1, one launch (start us, length us, event | category | flops | bytes accessed | tf_op | source)
XLA Modules:
  0.0 384.6 jit_solution(2428591143477013721)
XLA Ops:
  7.2 0.0 all-gather.3.cloned.1.call-start
  7.2 4.6 %collective-permute-start = (bf16[4,512,256]{2,1,0:T(8,128)(2,1)}, bf16[4,512,256]{2,1,0:T(8,128)(2,1)}, u32[]{:S(2)}, u32[]{:S(2)}) collective-permute-start(bf16[4,512,256]{2,1,0:T(8,128)(2,1)} %param.12), channel_id=1, source_target_pairs={{0,1},{1,2},{2,3},{3,4},{4,5},{5,6},{6,7},{8,9},{9,10},{10,11},{11... | collective-permute-start | bytes 3145736 | tf_op jit(solution)/shard_map/ppermute | solution.py:18
  11.8 1.9 collective-permute-start.1
  13.8 0.7 broadcast_subtract_fusion
  14.4 0.7 compare_select_fusion.5
  15.1 0.1 fusion.45
  15.2 0.0 copy-start.8
  15.2 3.4 copy_select_fusion
  18.6 5.2 %collective-permute-done = bf16[4,512,256]{2,1,0:T(8,128)(2,1)} collective-permute-done((bf16[4,512,256]{2,1,0:T(8,128)(2,1)}, bf16[4,512,256]{2,1,0:T(8,128)(2,1)}, u32[]{:S(2)}, u32[]{:S(2)}) %collective-permute-start) | collective-permute-done | bytes 1048608 | tf_op jit(solution)/shard_map/ppermute | solution.py:18
  23.9 1.3 constant_dynamic-update-slice_fusion.2
  25.1 0.0 copy-done.8
  25.2 0.1 constant_dynamic-update-slice_fusion.1
  25.2 3.0 collective-permute-done.1
  28.3 1.3 constant_dynamic-update-slice_fusion
  29.6 2.8 gather_fusion.1
  32.3 2.8 gather_fusion
  35.1 6.1 %fusion.10 = bf16[16,512,192]{1,2,0:T(8,128)(2,1)} fusion(bf16[16,512,256]{2,1,0:T(8,128)(2,1)} %gather_fusion.1, pred[16]{0:T(512)(128)(4,1)S(1)} %get-tuple-element.10, bf16[16,2,256,192]{2,3,0,1:T(8,128)(2,1)} %copy_select_fusion), kind=kOutput, calls=%fused_computation.22 | convolution fusion | flops 807403520 | bytes 8912912 | tf_op jit(solution)/shard_map/cyg,cgh->cyh/dot_general | solution.py:88
  41.2 0.0 copy-done.7
  41.2 7.3 %fusion.29 = f32[16,192,192]{2,1,0:T(8,128)} fusion(bf16[16,512,192]{1,2,0:T(8,128)(2,1)} %fusion.10, bf16[16,512,256]{2,1,0:T(8,128)(2,1)} %gather_fusion, pred[16]{0:T(512)(128)(4,1)S(1)} %get-tuple-element.6, bf16[16,2,256,192]{2,3,0,1:T(8,128)(2,1)S(1)} %copy-done.7), kind=kOutput, calls=%fused_computation.42 | convolution fusion | flops 1412956160 | bytes 11272704 | tf_op jit(solution)/shard_map/pqa,pqb->pab/dot_general | solution.py:94
  48.5 0.0 all-gather.3.cloned.1.call-update
  48.5 122.4 %all-gather.3.cloned.1.call-done = f32[64,192,192]{2,1,0:T(8,128)} async-done(((f32[16,192,192]{2,1,0:T(8,128)}), f32[64,192,192]{2,1,0:T(8,128)}) %all-gather.3.cloned.1.call-update) | async-done | bytes 9437200 | tf_op jit(solution)/shard_map/all_gather | solution.py:98
  170.9 6.2 %reduce_sum.9 = f32[16,192,192]{2,1,0:T(8,128)S(1)} reduce(f32[4,16,192,192]{3,2,1,0:T(8,128)} %bitcast.28, f32[]{:T(128)} %constant.29.clone.1), dimensions={0}, to_apply=%region_0.2 | reduce | flops 1769472 | bytes 11796484 | tf_op jit(solution)/shard_map/reduce_sum | solution.py:98
  177.1 0.0 copy-done.9
  177.1 0.0 copy-start.1
  177.1 0.0 copy-start.10
  177.1 0.0 copy-start.11
  177.1 2.4 fusion.17
  179.5 0.3 copy-done.1
  179.8 2.6 collective-permute-start.3
  182.3 3.2 collective-permute-start.2
  185.5 0.0 copy-done.10
  185.6 0.1 copy.19
  185.7 0.0 copy-done.11
  185.7 0.1 copy.24
  185.8 0.1 copy.20
  185.8 0.1 reshape.95
  185.9 32.8 %collective-permute-done.3 = f32[16,192,192]{2,1,0:T(8,128)} collective-permute-done((f32[16,192,192]{2,1,0:T(8,128)}, f32[16,192,192]{2,1,0:T(8,128)}, u32[]{:S(2)}, u32[]{:S(2)}) %collective-permute-start.3) | collective-permute-done | bytes 2359328 | tf_op jit(solution)/shard_map/ppermute | solution.py:20
  218.7 1.2 collective-permute-done.2
  219.9 7.7 %pad_maximum_fusion = f32[48,192,192]{2,1,0:T(8,128)} fusion(f32[16,192,192]{2,1,0:T(8,128)} %collective-permute-done.3, f32[16,192,192]{2,1,0:T(8,128)} %fusion.17, f32[16,192,192]{2,1,0:T(8,128)S(1)} %collective-permute-done.2), kind=kLoop, calls=%fused_computation.4 | loop fusion | flops 3538944 | bytes 14155776 | tf_op jit(solution)/shard_map/concatenate | solution.py:16
  227.6 7.4 %gather_fusion.2 = f32[32,192,192]{2,1,0:T(8,128)} fusion(f32[48,192,192]{2,1,0:T(8,128)} %pad_maximum_fusion, s32[1024]{0:T(1024)S(1)} %pad_clamp_fusion), kind=kCustom, calls=%fused_computation.1.clone | custom fusion | bytes 9437312 | tf_op jit(solution)/shard_map/jit(_take)/gather | solution.py:105
  235.0 0.0 copy-done
  235.0 9.5 %fusion.2 = f32[16,2,192,192]{3,2,1,0:T(8,128)S(1)} fusion(f32[16,2,192,192]{3,2,1,0:T(8,128)} %bitcast.27, bf16[16,2,192,192]{3,2,1,0:T(8,128)(2,1)S(1)} %copy-done, f32[16,192]{1,0:T(8,128)S(1)} %get-tuple-element.12, pred[16,2]{1,0:T(8,128)(4,1)S(1)} %copy.19), kind=kOutput, calls=%fused_computation.13 | convolution fusion | flops 2721447936 | bytes 11808800 | tf_op jit(solution)/shard_map/pnab,pnbc->pnac/dot_general | solution.py:41
  244.5 8.0 %fusion.5 = f32[16,2,192,192]{3,2,1,0:T(8,128)S(1)} fusion(f32[16,2,192,192]{3,2,1,0:T(8,128)S(1)} %fusion.2, bf16[16,2,192,192]{3,2,1,0:T(8,128)(2,1)S(1)} %copy-done, f32[16,192]{1,0:T(8,128)S(1)} %get-tuple-element.12), kind=kOutput, calls=%fused_computation.17 | convolution fusion | flops 2720268288 | bytes 11808768 | tf_op jit(solution)/shard_map/pnac,pndc->pnad/dot_general | solution.py:44
  252.6 0.0 copy-start.2
  252.6 23.4 %fusion.8 = f32[16,1,192,192]{3,1,2,0:T(1,128)S(1)} fusion(f32[16,2,1,1]{1,2,3,0:T(1,128)S(1)} %copy.24, f32[16,2,192,192]{3,2,1,0:T(8,128)S(1)} %fusion.5), kind=kOutput, calls=%fused_computation.20 | convolution fusion | flops 14155776 | bytes 7078016 | tf_op jit(solution)/shard_map/pn,pnad->pad/dot_general | solution.py:47
  276.0 0.0 copy-done.2
  276.0 1.4 fusion.20
  277.4 0.0 copy-start.4
  277.4 1.9 collective-permute-start.5
  279.3 0.0 copy-done.4
  279.3 4.3 %collective-permute-start.4 = (f32[16,192,192]{2,1,0:T(8,128)S(1)}, f32[16,192,192]{2,1,0:T(8,128)}, u32[]{:S(2)}, u32[]{:S(2)}) collective-permute-start(f32[16,192,192]{2,1,0:T(8,128)S(1)} %fusion.20), channel_id=1, source_target_pairs={{0,1},{1,2},{2,3},{3,4},{4,5},{5,6},{6,7},{8,9},{9,10},{10,11},{11... | collective-permute-start | bytes 7077896 | tf_op jit(solution)/shard_map/ppermute | solution.py:18
  283.6 33.0 %collective-permute-done.5 = f32[16,192,192]{2,1,0:T(8,128)S(1)} collective-permute-done((f32[16,192,192]{2,1,0:T(8,128)S(1)}, f32[16,192,192]{2,1,0:T(8,128)S(1)}, u32[]{:S(2)}, u32[]{:S(2)}) %collective-permute-start.5) | collective-permute-done | bytes 2359328 | tf_op jit(solution)/shard_map/ppermute | solution.py:20
  316.6 1.7 copy-done.6
  318.3 0.0 collective-permute-done.4
  318.3 8.5 %pad_maximum_fusion.1 = f32[48,192,192]{2,1,0:T(8,128)} fusion(f32[16,192,192]{2,1,0:T(8,128)} %copy-done.6, f32[16,192,192]{2,1,0:T(8,128)} %copy-done.4, f32[16,192,192]{2,1,0:T(8,128)} %collective-permute-done.4), kind=kLoop, calls=%fused_computation.5 | loop fusion | flops 3538944 | bytes 14155776 | tf_op jit(solution)/shard_map/concatenate | solution.py:16
  326.8 7.3 %gather_fusion.3 = f32[32,192,192]{2,1,0:T(8,128)} fusion(f32[48,192,192]{2,1,0:T(8,128)} %pad_maximum_fusion.1, s32[1024]{0:T(1024)S(1)} %pad_clamp_fusion), kind=kCustom, calls=%fused_computation.3.clone | custom fusion | bytes 9437312 | tf_op jit(solution)/shard_map/jit(_take)/gather | solution.py:105
  334.1 9.9 %fusion = f32[16,2,192,192]{3,2,1,0:T(8,128)S(1)} fusion(f32[16,2,192,192]{3,2,1,0:T(8,128)} %bitcast.26, bf16[16,2,192,192]{3,2,1,0:T(8,128)(2,1)S(1)} %copy-done, f32[16,192]{1,0:T(8,128)S(1)} %get-tuple-element.12, pred[16,2]{1,0:T(8,128)(4,1)S(1)} %copy.19), kind=kOutput, calls=%fused_computation.11 | convolution fusion | flops 2721447936 | bytes 11808800 | tf_op jit(solution)/shard_map/pnab,pnbc->pnac/dot_general | solution.py:41
  344.1 8.0 %fusion.4 = f32[16,2,192,192]{3,2,1,0:T(8,128)S(1)} fusion(f32[16,2,192,192]{3,2,1,0:T(8,128)S(1)} %fusion, bf16[16,2,192,192]{3,2,1,0:T(8,128)(2,1)S(1)} %copy-done, f32[16,192]{1,0:T(8,128)S(1)} %get-tuple-element.12), kind=kOutput, calls=%fused_computation.16 | convolution fusion | flops 2720268288 | bytes 11808768 | tf_op jit(solution)/shard_map/pnac,pndc->pnad/dot_general | solution.py:44
  352.1 0.0 copy-start.3
  352.1 0.0 copy-start.5
  352.1 23.3 %fusion.6 = f32[16,1,192,192]{3,1,2,0:T(1,128)S(1)} fusion(f32[16,2,1,1]{1,2,3,0:T(1,128)S(1)} %copy.24, f32[16,2,192,192]{3,2,1,0:T(8,128)S(1)} %fusion.4), kind=kOutput, calls=%fused_computation.18 | convolution fusion | flops 14155776 | bytes 7078016 | tf_op jit(solution)/shard_map/pn,pnad->pad/dot_general | solution.py:47
  375.5 0.0 copy-done.3
  375.5 0.0 copy-done.5
  375.5 2.0 fusion.22
  (8 shorter events, 0.0 us)
Async XLA Ops:
  7.2 163.7 %all-gather.3.cloned.1.call-start = ((), (), s32[]{:S(2)}) async-start(), calls=%async_computation | async-start | bytes 15728640 | tf_op jit(solution)/shard_map/all_gather | solution.py:98
  7.2 16.6 %collective-permute-start = (bf16[4,512,256]{2,1,0:T(8,128)(2,1)}, bf16[4,512,256]{2,1,0:T(8,128)(2,1)}, u32[]{:S(2)}, u32[]{:S(2)}) collective-permute-start(bf16[4,512,256]{2,1,0:T(8,128)(2,1)} %param.12), channel_id=1, source_target_pairs={{0,1},{1,2},{2,3},{3,4},{4,5},{5,6},{6,7},{8,9},{9,10},{10,11},{11... | collective-permute-start | bytes 3145736 | tf_op jit(solution)/shard_map/ppermute | solution.py:18
  11.8 16.4 %collective-permute-start.1 = (bf16[4,512,256]{2,1,0:T(8,128)(2,1)}, bf16[4,512,256]{2,1,0:T(8,128)(2,1)}, u32[]{:S(2)}, u32[]{:S(2)}) collective-permute-start(bf16[4,512,256]{2,1,0:T(8,128)(2,1)} %param.12), channel_id=1, source_target_pairs={{1,0},{2,1},{3,2},{4,3},{5,4},{6,5},{7,6},{9,8},{10,9},{11,10},{12... | collective-permute-start | bytes 3145736 | tf_op jit(solution)/shard_map/ppermute | solution.py:20
  15.2 10.0 %copy-start.8 = (bf16[4,512,256]{2,1,0:T(8,128)(2,1)S(1)}, bf16[4,512,256]{2,1,0:T(8,128)(2,1)}, u32[]{:S(2)}) copy-start(bf16[4,512,256]{2,1,0:T(8,128)(2,1)} %param.12) | copy-start | bytes 3145732
  35.1 6.1 %copy-start.7 = (bf16[16,2,256,192]{2,3,0,1:T(8,128)(2,1)S(1)}, bf16[16,2,256,192]{2,3,0,1:T(8,128)(2,1)}, u32[]{:S(2)}) copy-start(bf16[16,2,256,192]{2,3,0,1:T(8,128)(2,1)} %copy_select_fusion) | copy-start | bytes 9437188
  170.9 6.2 %copy-start.9 = (f32[16,192]{1,0:T(8,128)S(1)}, f32[16,192]{1,0:T(8,128)}, u32[]{:S(2)}) copy-start(f32[16,192]{1,0:T(8,128)} %param.16) | copy-start | bytes 36868
  177.1 2.7 copy-start.1
  177.1 8.4 %copy-start.10 = (s32[16,2]{0,1:T(2,128)S(1)}, s32[16,2]{0,1:T(2,128)}, u32[]{:S(2)}) copy-start(s32[16,2]{0,1:T(2,128)} %param.18) | copy-start | bytes 388
  177.1 8.5 %copy-start.11 = (f32[16,2]{0,1:T(2,128)S(1)}, f32[16,2]{0,1:T(2,128)}, u32[]{:S(2)}) copy-start(f32[16,2]{0,1:T(2,128)} %param.19) | copy-start | bytes 388
  179.8 38.9 %collective-permute-start.3 = (f32[16,192,192]{2,1,0:T(8,128)}, f32[16,192,192]{2,1,0:T(8,128)}, u32[]{:S(2)}, u32[]{:S(2)}) collective-permute-start(f32[16,192,192]{2,1,0:T(8,128)} %fusion.17), channel_id=1, source_target_pairs={{1,0},{2,1},{3,2},{4,3},{5,4},{6,5},{7,6},{9,8},{10,9},{11,10},{12... | collective-permute-start | bytes 7077896 | tf_op jit(solution)/shard_map/ppermute | solution.py:20
  182.3 37.5 %collective-permute-start.2 = (f32[16,192,192]{2,1,0:T(8,128)}, f32[16,192,192]{2,1,0:T(8,128)S(1)}, u32[]{:S(2)}, u32[]{:S(2)}) collective-permute-start(f32[16,192,192]{2,1,0:T(8,128)} %fusion.17), channel_id=1, source_target_pairs={{0,1},{1,2},{2,3},{3,4},{4,5},{5,6},{6,7},{8,9},{9,10},{10,11},{11... | collective-permute-start | bytes 7077896 | tf_op jit(solution)/shard_map/ppermute | solution.py:18
  227.5 7.5 %copy-start = (bf16[16,2,192,192]{3,2,1,0:T(8,128)(2,1)S(1)}, bf16[16,2,192,192]{3,2,1,0:T(8,128)(2,1)}, u32[]{:S(2)}) copy-start(bf16[16,2,192,192]{3,2,1,0:T(8,128)(2,1)} %param.17) | copy-start | bytes 7077892
  252.6 23.4 %copy-start.2 = (f32[16,192,192]{2,1,0:T(8,128)S(1)}, f32[16,192,192]{2,1,0:T(8,128)}, u32[]{:S(2)}) copy-start(f32[16,192,192]{2,1,0:T(8,128)} %copy-done.1) | copy-start | bytes 7077892
  277.4 1.9 copy-start.4
  277.4 39.2 %collective-permute-start.5 = (f32[16,192,192]{2,1,0:T(8,128)S(1)}, f32[16,192,192]{2,1,0:T(8,128)S(1)}, u32[]{:S(2)}, u32[]{:S(2)}) collective-permute-start(f32[16,192,192]{2,1,0:T(8,128)S(1)} %fusion.20), channel_id=1, source_target_pairs={{1,0},{2,1},{3,2},{4,3},{5,4},{6,5},{7,6},{9,8},{10,9},{11,10},{12... | collective-permute-start | bytes 7077896 | tf_op jit(solution)/shard_map/ppermute | solution.py:20
  279.3 39.0 %collective-permute-start.4 = (f32[16,192,192]{2,1,0:T(8,128)S(1)}, f32[16,192,192]{2,1,0:T(8,128)}, u32[]{:S(2)}, u32[]{:S(2)}) collective-permute-start(f32[16,192,192]{2,1,0:T(8,128)S(1)} %fusion.20), channel_id=1, source_target_pairs={{0,1},{1,2},{2,3},{3,4},{4,5},{5,6},{6,7},{8,9},{9,10},{10,11},{11... | collective-permute-start | bytes 7077896 | tf_op jit(solution)/shard_map/ppermute | solution.py:18
  316.6 1.7 copy-start.6
  352.1 23.4 %copy-start.3 = (f32[16,192,192]{2,1,0:T(8,128)S(1)}, f32[16,192,192]{2,1,0:T(8,128)}, u32[]{:S(2)}) copy-start(f32[16,192,192]{2,1,0:T(8,128)} %copy-done.1) | copy-start | bytes 7077892
  352.1 23.4 %copy-start.5 = (f32[16,192,192]{2,1,0:T(8,128)S(1)}, f32[16,192,192]{2,1,0:T(8,128)}, u32[]{:S(2)}) copy-start(f32[16,192,192]{2,1,0:T(8,128)} %copy-done.4) | copy-start | bytes 7077892
Sparse Core Ops, SparseCore 0:
  48.6 122.2 all-gather.2
